TPU v7x, 256 devices: a whole 4x4x8 slice. The times are simulated.
256 devices in a mesh: frame: 32 (over z, x_hi, core), head: 8 (over y, x_lo).
Axes of the slice: x: 4 (x_hi: 2, x_lo: 2; x = x_hi * 2 + x_lo), y: 4, z: 8, core: 2. Of those that a mesh axis runs over, the one named last changes fastest.
Arguments:
- query_vectors: bfloat16 [12288, 3072], P('frame', 'head'), may hold values from -17 to 17
- key_vectors: bfloat16 [12288, 3072], P('frame', 'head'), may hold values from -6 to 6
- value_vectors: bfloat16 [12288, 3072], P('frame', 'head'), may hold values from -6 to 6
- tile_mask: int32 [96, 96], replicated, may hold values from 0 to 1, as said below
- out_weight: bfloat16 [3072, 3072], P('head'), may hold values from -0.109375 to 0.109375
Outputs:
- projected: bfloat16 [12288, 3072], P(('frame', 'head'))
Inputs may be any that keep to these rules, and one draw needn't show every extreme that they name: The slab holds packed clips of whole tiles. Each clip lays its tiles out in order on a grid of latent frames by tile rows by tile columns. One clip spans 72 tiles and its latent frame holds 48 tiles, in 4 or 8 columns; every other clip has 2 to 4 rows and 2 to 4 columns, by clip. tile_mask[a, b] is 1 exactly when tiles a and b lie in the same clip and their frame, row and column indices each differ by at most 1.
All inputs are finite; a program needn't handle non-finite values.
Results may differ from a plain program's by a relative error of at most 0.02.
Values may be sent and summed in bfloat16 or wider, within the bound.
No kernel may reach another device: no remote copies, remote signals or barrier semaphores. Data moves between devices by JAX's collectives and lax.ppermute only.
A program may use at most 128 MiB of HBM per device.

v0:
```python
import functools
import math

import jax
import jax.numpy as jnp
from jax import lax
from jax.experimental import pallas as pl
from jax.experimental.pallas import tpu as pltpu
from jax.sharding import PartitionSpec as P

HD = 128
TILE = 128
MAX_KEYS = 27
KEYS_PER_STEP = 9


def key_lists(tile_rows):
    seen = jnp.cumsum((tile_rows > 0).astype(jnp.int32), axis=1)
    counts = jnp.minimum(seen[:, -1], MAX_KEYS)
    slots = jnp.arange(MAX_KEYS, dtype=jnp.int32)
    lists = jnp.sum((seen[:, None, :] <= slots[None, :, None]).astype(jnp.int32), axis=2)
    last = jnp.sum((seen <= (counts - 1)[:, None]).astype(jnp.int32), axis=1)
    lists = jnp.where(slots[None, :] < counts[:, None], lists, last[:, None])
    return lists.reshape(-1), counts


def attention_kernel(lists_ref, counts_ref, q_ref, *refs, head_count, scale):
    key_refs = refs[:KEYS_PER_STEP]
    value_refs = refs[KEYS_PER_STEP : 2 * KEYS_PER_STEP]
    o_ref = refs[2 * KEYS_PER_STEP]
    top_ref, total_ref, acc_ref = refs[2 * KEYS_PER_STEP + 1 :]
    tile = pl.program_id(0)
    step = pl.program_id(1)
    valid = counts_ref[tile] - step * KEYS_PER_STEP

    @pl.when(step == 0)
    def _():
        top_ref[...] = jnp.full(top_ref.shape, -jnp.inf, jnp.float32)
        total_ref[...] = jnp.zeros(total_ref.shape, jnp.float32)
        acc_ref[...] = jnp.zeros(acc_ref.shape, jnp.float32)

    @pl.when(valid > 0)
    def _():
        column = lax.broadcasted_iota(jnp.int32, (1, KEYS_PER_STEP * TILE), 1)
        in_list = column < valid * TILE
        for h in range(head_count):
            cols = pl.ds(h * HD, HD)
            q = q_ref[:, cols]
            k = jnp.concatenate([key_refs[j][:, cols] for j in range(KEYS_PER_STEP)], axis=0)
            v = jnp.concatenate([value_refs[j][:, cols] for j in range(KEYS_PER_STEP)], axis=0)
            s = lax.dot_general(
                q, k, (((1,), (1,)), ((), ())), preferred_element_type=jnp.float32
            ) * scale
            s = jnp.where(in_list, s, -jnp.inf)
            old_top = top_ref[h]
            new_top = jnp.maximum(old_top, jnp.max(s, axis=1, keepdims=True))
            weights = jnp.exp(s - new_top)
            factor = jnp.exp(old_top - new_top)
            total_ref[h] = total_ref[h] * factor + jnp.sum(weights, axis=1, keepdims=True)
            acc_ref[h] = acc_ref[h] * factor + jnp.dot(
                weights.astype(jnp.bfloat16), v, preferred_element_type=jnp.float32
            )
            top_ref[h] = new_top

    @pl.when(step == pl.num_programs(1) - 1)
    def _():
        for h in range(head_count):
            o_ref[:, pl.ds(h * HD, HD)] = (acc_ref[h] / total_ref[h]).astype(o_ref.dtype)


def sparse_attention(query_vectors, pair_piece, lists, counts):
    row_count, channels = query_vectors.shape
    head_count = channels // HD
    query_tiles = row_count // TILE
    steps = MAX_KEYS // KEYS_PER_STEP

    def key_spec(j, half):
        return pl.BlockSpec(
            (TILE, channels),
            lambda i, s, lists_ref, counts_ref: (
                lists_ref[i * MAX_KEYS + s * KEYS_PER_STEP + j],
                half,
            ),
        )

    row_spec = pl.BlockSpec((TILE, channels), lambda i, s, lists_ref, counts_ref: (i, 0))
    kernel = functools.partial(
        attention_kernel, head_count=head_count, scale=1.0 / math.sqrt(HD)
    )
    return pl.pallas_call(
        kernel,
        grid_spec=pltpu.PrefetchScalarGridSpec(
            num_scalar_prefetch=2,
            grid=(query_tiles, steps),
            in_specs=[row_spec]
            + [key_spec(j, 0) for j in range(KEYS_PER_STEP)]
            + [key_spec(j, 1) for j in range(KEYS_PER_STEP)],
            out_specs=row_spec,
            scratch_shapes=[
                pltpu.VMEM((head_count, TILE, 1), jnp.float32),
                pltpu.VMEM((head_count, TILE, 1), jnp.float32),
                pltpu.VMEM((head_count, TILE, HD), jnp.float32),
            ],
        ),
        out_shape=jax.ShapeDtypeStruct((row_count, channels), jnp.bfloat16),
        compiler_params=pltpu.CompilerParams(dimension_semantics=("arbitrary", "arbitrary")),
    )(lists, counts, query_vectors, *([pair_piece] * (2 * KEYS_PER_STEP)))


def shards(query_vectors, key_vectors, value_vectors, tile_mask, out_weight):
    row_count = query_vectors.shape[0]
    frame_pos = lax.axis_index("frame")
    tiles_here = row_count // TILE
    query_tiles = lax.dynamic_slice_in_dim(tile_mask, frame_pos * tiles_here, tiles_here, 0)
    lists, counts = key_lists(query_tiles)
    pair_piece = lax.all_gather(
        jnp.concatenate([key_vectors, value_vectors], axis=1), "frame", axis=0, tiled=True
    )
    attended = sparse_attention(query_vectors, pair_piece, lists, counts)
    partial = jnp.dot(attended, out_weight, preferred_element_type=jnp.float32).astype(jnp.bfloat16)
    head_count = lax.axis_size("head")
    pieces = lax.all_to_all(
        partial.reshape(head_count, row_count // head_count, partial.shape[1]), "head", 0, 0
    )
    return jnp.sum(pieces.astype(jnp.float32), axis=0).astype(jnp.bfloat16)


def solution(mesh):
    in_specs = (P("frame", "head"), P("frame", "head"), P("frame", "head"), P(), P("head", None))
    out_specs = P(("frame", "head"), None)
    return jax.shard_map(shards, mesh=mesh, in_specs=in_specs, out_specs=out_specs, check_vma=False)
```

profile of v0, /device:TPU:1, one launch (start us, length us, event | category | flops | bytes accessed | tf_op | source)
XLA Modules:
  0.0 221.0 jit_solution(15077652649563237352)
XLA Ops:
  6.5 0.0 copy-start
  6.5 0.0 all-gather.2.cloned.1.call-start
  6.5 2.1 pad_maximum_fusion
  8.6 0.0 all-gather.2.cloned.1.call-update
  8.6 0.7 fusion.1
  9.3 0.3 reduce_window_sum.11
  9.6 0.2 fusion.2
  9.8 0.0 copy-start.1
  9.8 0.1 convert_reduce_fusion
  10.0 0.2 convert_reduce_fusion.1
  10.1 0.1 fusion
  10.2 0.7 select_n.13.lists_ref
  10.9 151.3 %all-gather.2.cloned.1.call-done.refs_0_.refs_1_.refs_2_.refs_3_.refs_4_.refs_5_.refs_6_.refs_7_.refs_8_.refs_9_.refs_10_.refs_11_.refs_12_.refs_13_.refs_14_.refs_15_.refs_16_.refs_17_ = bf16[12288,768]{1,0:T(8,128)(2,1)} async-done(((bf16[384,768]{1,0:T(8,128)(2,1)}), bf16[12288,768]{1,0:T(8,128)(2,1)}) %all-gather.2.cloned.1.call-update) | async-done | bytes 18874384 | tf_op jit(solution)/shard_map/all_gather | solution.py:116
  162.2 0.0 copy-done.1
  162.2 13.5 %shard_map.55 = bf16[384,384]{1,0:T(8,128)(2,1)} custom-call(s32[81]{0:T(128)} %select_n.13.lists_ref, s32[3]{0:T(128)} %copy-done.1, bf16[384,384]{1,0:T(8,128)(2,1)} %q_ref.1, ...), custom_call_target="tpu_custom_call" | custom-call | tf_op jit(solution)/shard_map/pallas_call | solution.py:90
  175.6 0.0 copy-done
  175.6 2.3 %convolution_convert_fusion = bf16[384,3072]{1,0:T(8,128)(2,1)S(1)} fusion(bf16[384,384]{1,0:T(8,128)(2,1)} %shard_map.55, bf16[384,3072]{1,0:T(8,128)(2,1)S(1)} %copy-done), kind=kOutput, calls=%fused_computation | convolution fusion | flops 907149312 | bytes 5013504 | tf_op jit(solution)/shard_map/dot_general | solution.py:120
  178.0 33.3 %all_to_all.5 = bf16[8,48,3072]{2,1,0:T(8,128)(2,1)} all-to-all(bf16[8,48,3072]{2,1,0:T(8,128)(2,1)S(1)} %bitcast.3), channel_id=1, replica_groups=mesh['frame'=32,'head'=8] {'head'}, dimensions={0} | all-to-all | bytes 4718592 | tf_op jit(solution)/shard_map/all_to_all | solution.py:122
  211.3 2.8 %reduce_sum.32 = bf16[48,3072]{1,0:T(8,128)(2,1)} reduce(bf16[8,48,3072]{2,1,0:T(8,128)(2,1)} %all_to_all.5, bf16[]{:T(256)} %constant.23.clone.1), dimensions={0}, to_apply=%region_3.4 | reduce | flops 1032192 | bytes 2654210 | tf_op jit(solution)/shard_map/reduce_sum | solution.py:125
Async XLA Ops:
  6.5 169.1 %copy-start = (bf16[384,3072]{1,0:T(8,128)(2,1)S(1)}, bf16[384,3072]{1,0:T(8,128)(2,1)}, u32[]{:S(2)}) copy-start(bf16[384,3072]{1,0:T(8,128)(2,1)} %param.9) | copy-start | bytes 7077892
  6.5 155.6 %all-gather.2.cloned.1.call-start = ((), (), s32[]{:S(2)}) async-start(), calls=%async_computation.1 | async-start | bytes 19464192 | tf_op jit(solution)/shard_map/all_gather | solution.py:116
  9.8 152.3 %copy-start.1 = (s32[3]{0:T(128)}, s32[3]{0:T(128)S(1)}, u32[]{:S(2)}) copy-start(s32[3]{0:T(128)S(1)} %get-tuple-element.5.counts_ref) | copy-start | bytes 40
Sparse Core Ops, SparseCore 0:
  10.1 152.0 all-gather.1
where the time goes:
time: 223 us; the launch traced here: 221 us
  waiting for transfers between devices  151 us (68%)
  blocking collectives  33.3 us (15%)
  Pallas kernels  13.5 us (6%)
  between operations  13.4 us (6%)
  other arithmetic  6.44 us (3%)
  matrix products  2.35 us (1%)
    all_gather x1, waiting for transfers between devices, shards(): lax.all_gather(jnp.concatenate([key_vectors, value_vectors], axis=1), 'fr...  151 us
    all_to_all x1, blocking collectives, shards(): lax.all_to_all(partial.reshape(head_count, row_count // head_count, parti...  33.3 us
    pallas_call x1, Pallas kernels, sparse_attention(): pl.pallas_call(kernel, grid_spec=pltpu.PrefetchScalarGridSpec(num_scalar_...  13.5 us
  transfers between devices with their start and end apart: 1, of which 1 were waited for; matrix products, arithmetic and copies ran while one was open for 1% of the time, Pallas kernels for 0%

commit v1 on v0

--- a/solution.py
+++ b/solution.py
@@ -27,8 +27,8 @@
 def attention_kernel(lists_ref, counts_ref, q_ref, *refs, head_count, scale):
     key_refs = refs[:KEYS_PER_STEP]
     value_refs = refs[KEYS_PER_STEP : 2 * KEYS_PER_STEP]
-    o_ref = refs[2 * KEYS_PER_STEP]
-    top_ref, total_ref, acc_ref = refs[2 * KEYS_PER_STEP + 1 :]
+    w_ref, o_ref = refs[2 * KEYS_PER_STEP : 2 * KEYS_PER_STEP + 2]
+    top_ref, total_ref, acc_ref = refs[2 * KEYS_PER_STEP + 2 :]
     tile = pl.program_id(0)
     step = pl.program_id(1)
     valid = counts_ref[tile] - step * KEYS_PER_STEP
@@ -39,8 +39,7 @@
         total_ref[...] = jnp.zeros(total_ref.shape, jnp.float32)
         acc_ref[...] = jnp.zeros(acc_ref.shape, jnp.float32)
 
-    @pl.when(valid > 0)
-    def _():
+    def update(masked):
         column = lax.broadcasted_iota(jnp.int32, (1, KEYS_PER_STEP * TILE), 1)
         in_list = column < valid * TILE
         for h in range(head_count):
@@ -51,7 +50,8 @@
             s = lax.dot_general(
                 q, k, (((1,), (1,)), ((), ())), preferred_element_type=jnp.float32
             ) * scale
-            s = jnp.where(in_list, s, -jnp.inf)
+            if masked:
+                s = jnp.where(in_list, s, -jnp.inf)
             old_top = top_ref[h]
             new_top = jnp.maximum(old_top, jnp.max(s, axis=1, keepdims=True))
             weights = jnp.exp(s - new_top)
@@ -62,13 +62,25 @@
             )
             top_ref[h] = new_top
 
+    @pl.when(valid >= KEYS_PER_STEP)
+    def _():
+        update(False)
+
+    @pl.when((valid > 0) & (valid < KEYS_PER_STEP))
+    def _():
+        update(True)
+
     @pl.when(step == pl.num_programs(1) - 1)
     def _():
-        for h in range(head_count):
-            o_ref[:, pl.ds(h * HD, HD)] = (acc_ref[h] / total_ref[h]).astype(o_ref.dtype)
+        attended = jnp.concatenate(
+            [(acc_ref[h] / total_ref[h]).astype(jnp.bfloat16) for h in range(head_count)], axis=1
+        )
+        o_ref[...] = jnp.dot(attended, w_ref[...], preferred_element_type=jnp.float32).astype(
+            o_ref.dtype
+        )
 
 
-def sparse_attention(query_vectors, pair_piece, lists, counts):
+def sparse_attention(query_vectors, pair_piece, out_weight, lists, counts):
     row_count, channels = query_vectors.shape
     head_count = channels // HD
     query_tiles = row_count // TILE
@@ -94,17 +106,20 @@
             grid=(query_tiles, steps),
             in_specs=[row_spec]
             + [key_spec(j, 0) for j in range(KEYS_PER_STEP)]
-            + [key_spec(j, 1) for j in range(KEYS_PER_STEP)],
-            out_specs=row_spec,
+            + [key_spec(j, 1) for j in range(KEYS_PER_STEP)]
+            + [pl.BlockSpec(out_weight.shape, lambda i, s, lists_ref, counts_ref: (0, 0))],
+            out_specs=pl.BlockSpec(
+                (TILE, out_weight.shape[1]), lambda i, s, lists_ref, counts_ref: (i, 0)
+            ),
             scratch_shapes=[
                 pltpu.VMEM((head_count, TILE, 1), jnp.float32),
                 pltpu.VMEM((head_count, TILE, 1), jnp.float32),
                 pltpu.VMEM((head_count, TILE, HD), jnp.float32),
             ],
         ),
-        out_shape=jax.ShapeDtypeStruct((row_count, channels), jnp.bfloat16),
+        out_shape=jax.ShapeDtypeStruct((row_count, out_weight.shape[1]), jnp.bfloat16),
         compiler_params=pltpu.CompilerParams(dimension_semantics=("arbitrary", "arbitrary")),
-    )(lists, counts, query_vectors, *([pair_piece] * (2 * KEYS_PER_STEP)))
+    )(lists, counts, query_vectors, *([pair_piece] * (2 * KEYS_PER_STEP)), out_weight)
 
 
 def shards(query_vectors, key_vectors, value_vectors, tile_mask, out_weight):
@@ -116,8 +131,7 @@
     pair_piece = lax.all_gather(
         jnp.concatenate([key_vectors, value_vectors], axis=1), "frame", axis=0, tiled=True
     )
-    attended = sparse_attention(query_vectors, pair_piece, lists, counts)
-    partial = jnp.dot(attended, out_weight, preferred_element_type=jnp.float32).astype(jnp.bfloat16)
+    partial = sparse_attention(query_vectors, pair_piece, out_weight, lists, counts)
     head_count = lax.axis_size("head")
     pieces = lax.all_to_all(
         partial.reshape(head_count, row_count // head_count, partial.shape[1]), "head", 0, 0

time: 223 us -> 221 us (level)
  matrix products: 2.35 us -> 0 us
    dot_general x1 -> x0, matrix products: 2.35 us -> none  [shards(): jnp.dot(attended, out_weight, preferred_element_type=jnp.float32)]
where the time goes in v1:
time: 221 us; the launch traced here: 218 us
  waiting for transfers between devices  151 us (68%)
  blocking collectives  32.9 us (15%)
  Pallas kernels  14.8 us (7%)
  between operations  13.4 us (6%)
  other arithmetic  4.62 us (2%)
    all_gather x1, waiting for transfers between devices, shards(): lax.all_gather(jnp.concatenate([key_vectors, value_vectors], axis=1), 'fr...  151 us
    all_to_all x1, blocking collectives, shards(): lax.all_to_all(partial.reshape(head_count, row_count // head_count, parti...  32.9 us
    pallas_call x1, Pallas kernels, sparse_attention(): pl.pallas_call(kernel, grid_spec=pltpu.PrefetchScalarGridSpec(num_scalar_...  14.8 us
  transfers between devices with their start and end apart: 1, of which 1 were waited for; matrix products, arithmetic and copies ran while one was open for 1% of the time, Pallas kernels for 0%

profile of v1, /device:TPU:1, one launch (start us, length us, event | category | flops | bytes accessed | tf_op | source)
XLA Modules:
  0.0 217.8 jit_solution(15550570490929702352)
XLA Ops:
  6.5 0.0 all-gather.2.cloned.1.call-start
  6.5 1.9 pad_maximum_fusion
  8.5 0.0 all-gather.2.cloned.1.call-update
  8.5 0.7 fusion.1
  9.2 0.3 reduce_window_sum.11
  9.5 0.2 fusion.2
  9.7 0.0 copy-start
  9.7 0.1 convert_reduce_fusion
  9.8 0.2 convert_reduce_fusion.1
  10.0 0.1 fusion
  10.1 0.6 select_n.13.lists_ref
  10.7 151.5 %all-gather.2.cloned.1.call-done.refs_0_.refs_1_.refs_2_.refs_3_.refs_4_.refs_5_.refs_6_.refs_7_.refs_8_.refs_9_.refs_10_.refs_11_.refs_12_.refs_13_.refs_14_.refs_15_.refs_16_.refs_17_ = bf16[12288,768]{1,0:T(8,128)(2,1)} async-done(((bf16[384,768]{1,0:T(8,128)(2,1)}), bf16[12288,768]{1,0:T(8,128)(2,1)}) %all-gather.2.cloned.1.call-update) | async-done | bytes 18874384 | tf_op jit(solution)/shard_map/all_gather | solution.py:131
  162.2 0.0 copy-done
  162.2 14.8 %shard_map.55 = bf16[384,3072]{1,0:T(8,128)(2,1)} custom-call(s32[81]{0:T(128)} %select_n.13.lists_ref, s32[3]{0:T(128)} %copy-done, bf16[384,384]{1,0:T(8,128)(2,1)} %q_ref.1, ...), custom_call_target="tpu_custom_call" | custom-call | tf_op jit(solution)/shard_map/pallas_call | solution.py:102
  176.9 32.9 %all_to_all.5 = bf16[8,48,3072]{2,1,0:T(8,128)(2,1)S(1)} all-to-all(bf16[8,48,3072]{2,1,0:T(8,128)(2,1)} %bitcast.1), channel_id=1, replica_groups=mesh['frame'=32,'head'=8] {'head'}, dimensions={0} | all-to-all | bytes 4718592 | tf_op jit(solution)/shard_map/all_to_all | solution.py:136
  209.8 1.1 reduce_sum.32
Async XLA Ops:
  6.5 155.6 %all-gather.2.cloned.1.call-start = ((), (), s32[]{:S(2)}) async-start(), calls=%async_computation.1 | async-start | bytes 19464192 | tf_op jit(solution)/shard_map/all_gather | solution.py:131
  9.7 152.5 %copy-start = (s32[3]{0:T(128)}, s32[3]{0:T(128)S(1)}, u32[]{:S(2)}) copy-start(s32[3]{0:T(128)S(1)} %get-tuple-element.5.counts_ref) | copy-start | bytes 40
Sparse Core Ops, SparseCore 0:
  10.1 152.0 all-gather.1

commit v2 on v1

--- a/solution.py
+++ b/solution.py
@@ -40,26 +40,38 @@
         acc_ref[...] = jnp.zeros(acc_ref.shape, jnp.float32)
 
     def update(masked):
-        column = lax.broadcasted_iota(jnp.int32, (1, KEYS_PER_STEP * TILE), 1)
-        in_list = column < valid * TILE
         for h in range(head_count):
             cols = pl.ds(h * HD, HD)
             q = q_ref[:, cols]
-            k = jnp.concatenate([key_refs[j][:, cols] for j in range(KEYS_PER_STEP)], axis=0)
-            v = jnp.concatenate([value_refs[j][:, cols] for j in range(KEYS_PER_STEP)], axis=0)
-            s = lax.dot_general(
-                q, k, (((1,), (1,)), ((), ())), preferred_element_type=jnp.float32
-            ) * scale
-            if masked:
-                s = jnp.where(in_list, s, -jnp.inf)
+
+            def scores(j):
+                s = lax.dot_general(
+                    q, key_refs[j][:, cols], (((1,), (1,)), ((), ())),
+                    preferred_element_type=jnp.float32,
+                ) * scale
+                return s
+
             old_top = top_ref[h]
-            new_top = jnp.maximum(old_top, jnp.max(s, axis=1, keepdims=True))
-            weights = jnp.exp(s - new_top)
+            new_top = old_top
+            for j in range(KEYS_PER_STEP):
+                row_max = jnp.max(scores(j), axis=1, keepdims=True)
+                if masked:
+                    row_max = jnp.where(j < valid, row_max, -jnp.inf)
+                new_top = jnp.maximum(new_top, row_max)
             factor = jnp.exp(old_top - new_top)
-            total_ref[h] = total_ref[h] * factor + jnp.sum(weights, axis=1, keepdims=True)
-            acc_ref[h] = acc_ref[h] * factor + jnp.dot(
-                weights.astype(jnp.bfloat16), v, preferred_element_type=jnp.float32
-            )
+            total = total_ref[h] * factor
+            acc = acc_ref[h] * factor
+            for j in range(KEYS_PER_STEP):
+                weights = jnp.exp(scores(j) - new_top)
+                if masked:
+                    weights = jnp.where(j < valid, weights, 0.0)
+                total = total + jnp.sum(weights, axis=1, keepdims=True)
+                acc = acc + jnp.dot(
+                    weights.astype(jnp.bfloat16), value_refs[j][:, cols],
+                    preferred_element_type=jnp.float32,
+                )
+            total_ref[h] = total
+            acc_ref[h] = acc
             top_ref[h] = new_top
 
     @pl.when(valid >= KEYS_PER_STEP)

time: 221 us -> 223 us (level)
  no operation moved by 1% of the time
where the time goes in v2:
time: 223 us; the launch traced here: 220 us
  waiting for transfers between devices  151 us (68%)
  blocking collectives  33.6 us (15%)
  Pallas kernels  16.1 us (7%)
  between operations  13.4 us (6%)
  other arithmetic  4.62 us (2%)
    all_gather x1, waiting for transfers between devices, shards(): lax.all_gather(jnp.concatenate([key_vectors, value_vectors], axis=1), 'fr...  151 us
    all_to_all x1, blocking collectives, shards(): lax.all_to_all(partial.reshape(head_count, row_count // head_count, parti...  33.6 us
    pallas_call x1, Pallas kernels, sparse_attention(): pl.pallas_call(kernel, grid_spec=pltpu.PrefetchScalarGridSpec(num_scalar_...  16.1 us
  transfers between devices with their start and end apart: 1, of which 1 were waited for; matrix products, arithmetic and copies ran while one was open for 1% of the time, Pallas kernels for 0%

profile of v2, /device:TPU:1, one launch (start us, length us, event | category | flops | bytes accessed | tf_op | source)
XLA Modules:
  0.0 219.9 jit_solution(15887087911782007832)
XLA Ops:
  6.5 0.0 all-gather.2.cloned.1.call-start
  6.5 1.9 pad_maximum_fusion
  8.5 0.0 all-gather.2.cloned.1.call-update
  8.5 0.7 fusion.1
  9.2 0.3 reduce_window_sum.11
  9.5 0.2 fusion.2
  9.7 0.0 copy-start
  9.7 0.1 convert_reduce_fusion
  9.8 0.2 convert_reduce_fusion.1
  10.0 0.1 fusion
  10.1 0.6 select_n.13.lists_ref
  10.7 151.5 %all-gather.2.cloned.1.call-done.refs_0_.refs_1_.refs_2_.refs_3_.refs_4_.refs_5_.refs_6_.refs_7_.refs_8_.refs_9_.refs_10_.refs_11_.refs_12_.refs_13_.refs_14_.refs_15_.refs_16_.refs_17_ = bf16[12288,768]{1,0:T(8,128)(2,1)} async-done(((bf16[384,768]{1,0:T(8,128)(2,1)}), bf16[12288,768]{1,0:T(8,128)(2,1)}) %all-gather.2.cloned.1.call-update) | async-done | bytes 18874384 | tf_op jit(solution)/shard_map/all_gather | solution.py:143
  162.2 0.0 copy-done
  162.2 16.1 %shard_map.55 = bf16[384,3072]{1,0:T(8,128)(2,1)} custom-call(s32[81]{0:T(128)} %select_n.13.lists_ref, s32[3]{0:T(128)} %copy-done, bf16[384,384]{1,0:T(8,128)(2,1)} %q_ref.1, ...), custom_call_target="tpu_custom_call" | custom-call | tf_op jit(solution)/shard_map/pallas_call | solution.py:114
  178.3 33.6 %all_to_all.5 = bf16[8,48,3072]{2,1,0:T(8,128)(2,1)S(1)} all-to-all(bf16[8,48,3072]{2,1,0:T(8,128)(2,1)} %bitcast.1), channel_id=1, replica_groups=mesh['frame'=32,'head'=8] {'head'}, dimensions={0} | all-to-all | bytes 4718592 | tf_op jit(solution)/shard_map/all_to_all | solution.py:148
  211.9 1.1 reduce_sum.32
Async XLA Ops:
  6.5 155.6 %all-gather.2.cloned.1.call-start = ((), (), s32[]{:S(2)}) async-start(), calls=%async_computation.1 | async-start | bytes 19464192 | tf_op jit(solution)/shard_map/all_gather | solution.py:143
  9.7 152.5 %copy-start = (s32[3]{0:T(128)}, s32[3]{0:T(128)S(1)}, u32[]{:S(2)}) copy-start(s32[3]{0:T(128)S(1)} %get-tuple-element.5.counts_ref) | copy-start | bytes 40
Sparse Core Ops, SparseCore 0:
  10.1 152.0 all-gather.1

commit v3 on v1

--- a/solution.py
+++ b/solution.py
@@ -25,10 +25,10 @@
 
 
 def attention_kernel(lists_ref, counts_ref, q_ref, *refs, head_count, scale):
-    key_refs = refs[:KEYS_PER_STEP]
-    value_refs = refs[KEYS_PER_STEP : 2 * KEYS_PER_STEP]
-    w_ref, o_ref = refs[2 * KEYS_PER_STEP : 2 * KEYS_PER_STEP + 2]
-    top_ref, total_ref, acc_ref = refs[2 * KEYS_PER_STEP + 2 :]
+    pair_refs = refs[:KEYS_PER_STEP]
+    w_ref, o_ref = refs[KEYS_PER_STEP : KEYS_PER_STEP + 2]
+    top_ref, total_ref, acc_ref = refs[KEYS_PER_STEP + 2 :]
+    channels = q_ref.shape[1]
     tile = pl.program_id(0)
     step = pl.program_id(1)
     valid = counts_ref[tile] - step * KEYS_PER_STEP
@@ -45,8 +45,9 @@
         for h in range(head_count):
             cols = pl.ds(h * HD, HD)
             q = q_ref[:, cols]
-            k = jnp.concatenate([key_refs[j][:, cols] for j in range(KEYS_PER_STEP)], axis=0)
-            v = jnp.concatenate([value_refs[j][:, cols] for j in range(KEYS_PER_STEP)], axis=0)
+            value_cols = pl.ds(channels + h * HD, HD)
+            k = jnp.concatenate([pair_refs[j][:, cols] for j in range(KEYS_PER_STEP)], axis=0)
+            v = jnp.concatenate([pair_refs[j][:, value_cols] for j in range(KEYS_PER_STEP)], axis=0)
             s = lax.dot_general(
                 q, k, (((1,), (1,)), ((), ())), preferred_element_type=jnp.float32
             ) * scale
@@ -86,12 +87,12 @@
     query_tiles = row_count // TILE
     steps = MAX_KEYS // KEYS_PER_STEP
 
-    def key_spec(j, half):
+    def key_spec(j):
         return pl.BlockSpec(
-            (TILE, channels),
+            (TILE, 2 * channels),
             lambda i, s, lists_ref, counts_ref: (
                 lists_ref[i * MAX_KEYS + s * KEYS_PER_STEP + j],
-                half,
+                0,
             ),
         )
 
@@ -105,8 +106,7 @@
             num_scalar_prefetch=2,
             grid=(query_tiles, steps),
             in_specs=[row_spec]
-            + [key_spec(j, 0) for j in range(KEYS_PER_STEP)]
-            + [key_spec(j, 1) for j in range(KEYS_PER_STEP)]
+            + [key_spec(j) for j in range(KEYS_PER_STEP)]
             + [pl.BlockSpec(out_weight.shape, lambda i, s, lists_ref, counts_ref: (0, 0))],
             out_specs=pl.BlockSpec(
                 (TILE, out_weight.shape[1]), lambda i, s, lists_ref, counts_ref: (i, 0)
@@ -119,7 +119,7 @@
         ),
         out_shape=jax.ShapeDtypeStruct((row_count, out_weight.shape[1]), jnp.bfloat16),
         compiler_params=pltpu.CompilerParams(dimension_semantics=("arbitrary", "arbitrary")),
-    )(lists, counts, query_vectors, *([pair_piece] * (2 * KEYS_PER_STEP)), out_weight)
+    )(lists, counts, query_vectors, *([pair_piece] * KEYS_PER_STEP), out_weight)
 
 
 def shards(query_vectors, key_vectors, value_vectors, tile_mask, out_weight):

time: 221 us -> 220 us (level); the launches traced: 218 us -> 219 us
  no operation moved by 1% of the time
where the time goes in v3:
time: 220 us; the launch traced here: 219 us
  waiting for transfers between devices  151 us (69%)
  blocking collectives  33.6 us (15%)
  Pallas kernels  15.5 us (7%)
  between operations  13.4 us (6%)
  other arithmetic  4.62 us (2%)
    all_gather x1, waiting for transfers between devices, shards(): lax.all_gather(jnp.concatenate([key_vectors, value_vectors], axis=1), 'fr...  151 us
    all_to_all x1, blocking collectives, shards(): lax.all_to_all(partial.reshape(head_count, row_count // head_count, parti...  33.6 us
    pallas_call x1, Pallas kernels, sparse_attention(): pl.pallas_call(kernel, grid_spec=pltpu.PrefetchScalarGridSpec(num_scalar_...  15.5 us
  transfers between devices with their start and end apart: 1, of which 1 were waited for; matrix products, arithmetic and copies ran while one was open for 1% of the time, Pallas kernels for 0%

profile of v3, /device:TPU:1, one launch (start us, length us, event | category | flops | bytes accessed | tf_op | source)
XLA Modules:
  0.0 219.2 jit_solution(17936444633560636435)
XLA Ops:
  6.5 0.0 all-gather.2.cloned.1.call-start
  6.5 1.9 pad_maximum_fusion
  8.5 0.0 all-gather.2.cloned.1.call-update
  8.5 0.7 fusion.1
  9.2 0.3 reduce_window_sum.11
  9.5 0.2 fusion.2
  9.7 0.0 copy-start
  9.7 0.1 convert_reduce_fusion
  9.8 0.2 convert_reduce_fusion.1
  10.0 0.1 fusion
  10.1 0.6 select_n.13.lists_ref
  10.7 151.5 %all-gather.2.cloned.1.call-done.refs_0_.refs_1_.refs_2_.refs_3_.refs_4_.refs_5_.refs_6_.refs_7_.refs_8_ = bf16[12288,768]{1,0:T(8,128)(2,1)} async-done(((bf16[384,768]{1,0:T(8,128)(2,1)}), bf16[12288,768]{1,0:T(8,128)(2,1)}) %all-gather.2.cloned.1.call-update) | async-done | bytes 18874384 | tf_op jit(solution)/shard_map/all_gather | solution.py:131
  162.2 0.0 copy-done
  162.2 15.5 %shard_map.55 = bf16[384,3072]{1,0:T(8,128)(2,1)} custom-call(s32[81]{0:T(128)} %select_n.13.lists_ref, s32[3]{0:T(128)} %copy-done, bf16[384,384]{1,0:T(8,128)(2,1)} %q_ref.1, bf16[12288,768]{1,0:T(8,128)(2,1)} %all-gather.2.cloned.1.call-done.refs_0_.refs_1_.refs_2_.refs_3_.refs_4_.refs_5_.refs_6_.refs_7_.refs_8_, ...), custom_call_target="tpu_custom_call" | custom-call | tf_op jit(solution)/shard_map/pallas_call | solution.py:103
  177.6 33.6 %all_to_all.5 = bf16[8,48,3072]{2,1,0:T(8,128)(2,1)S(1)} all-to-all(bf16[8,48,3072]{2,1,0:T(8,128)(2,1)} %bitcast.1), channel_id=1, replica_groups=mesh['frame'=32,'head'=8] {'head'}, dimensions={0} | all-to-all | bytes 4718592 | tf_op jit(solution)/shard_map/all_to_all | solution.py:136
  211.2 1.1 reduce_sum.32
Async XLA Ops:
  6.5 155.6 %all-gather.2.cloned.1.call-start = ((), (), s32[]{:S(2)}) async-start(), calls=%async_computation.1 | async-start | bytes 19464192 | tf_op jit(solution)/shard_map/all_gather | solution.py:131
  9.7 152.5 %copy-start = (s32[3]{0:T(128)}, s32[3]{0:T(128)S(1)}, u32[]{:S(2)}) copy-start(s32[3]{0:T(128)S(1)} %get-tuple-element.5.counts_ref) | copy-start | bytes 40
Sparse Core Ops, SparseCore 0:
  10.1 152.0 all-gather.1

commit v4 on v1

--- a/solution.py
+++ b/solution.py
@@ -40,25 +40,26 @@
         acc_ref[...] = jnp.zeros(acc_ref.shape, jnp.float32)
 
     def update(masked):
-        column = lax.broadcasted_iota(jnp.int32, (1, KEYS_PER_STEP * TILE), 1)
-        in_list = column < valid * TILE
+        row = lax.broadcasted_iota(jnp.int32, (KEYS_PER_STEP * TILE, 1), 0)
+        in_list = row < valid * TILE
         for h in range(head_count):
             cols = pl.ds(h * HD, HD)
             q = q_ref[:, cols]
             k = jnp.concatenate([key_refs[j][:, cols] for j in range(KEYS_PER_STEP)], axis=0)
             v = jnp.concatenate([value_refs[j][:, cols] for j in range(KEYS_PER_STEP)], axis=0)
             s = lax.dot_general(
-                q, k, (((1,), (1,)), ((), ())), preferred_element_type=jnp.float32
+                k, q, (((1,), (1,)), ((), ())), preferred_element_type=jnp.float32
             ) * scale
             if masked:
                 s = jnp.where(in_list, s, -jnp.inf)
             old_top = top_ref[h]
-            new_top = jnp.maximum(old_top, jnp.max(s, axis=1, keepdims=True))
+            new_top = jnp.maximum(old_top, jnp.max(s, axis=0, keepdims=True))
             weights = jnp.exp(s - new_top)
             factor = jnp.exp(old_top - new_top)
-            total_ref[h] = total_ref[h] * factor + jnp.sum(weights, axis=1, keepdims=True)
-            acc_ref[h] = acc_ref[h] * factor + jnp.dot(
-                weights.astype(jnp.bfloat16), v, preferred_element_type=jnp.float32
+            total_ref[h] = total_ref[h] * factor + jnp.sum(weights, axis=0, keepdims=True)
+            acc_ref[h] = acc_ref[h] * factor + lax.dot_general(
+                v, weights.astype(jnp.bfloat16), (((0,), (0,)), ((), ())),
+                preferred_element_type=jnp.float32,
             )
             top_ref[h] = new_top
 
@@ -73,7 +74,7 @@
     @pl.when(step == pl.num_programs(1) - 1)
     def _():
         attended = jnp.concatenate(
-            [(acc_ref[h] / total_ref[h]).astype(jnp.bfloat16) for h in range(head_count)], axis=1
+            [(acc_ref[h] / total_ref[h]).T.astype(jnp.bfloat16) for h in range(head_count)], axis=1
         )
         o_ref[...] = jnp.dot(attended, w_ref[...], preferred_element_type=jnp.float32).astype(
             o_ref.dtype
@@ -112,8 +113,8 @@
                 (TILE, out_weight.shape[1]), lambda i, s, lists_ref, counts_ref: (i, 0)
             ),
             scratch_shapes=[
-                pltpu.VMEM((head_count, TILE, 1), jnp.float32),
-                pltpu.VMEM((head_count, TILE, 1), jnp.float32),
+                pltpu.VMEM((head_count, 1, TILE), jnp.float32),
+                pltpu.VMEM((head_count, 1, TILE), jnp.float32),
                 pltpu.VMEM((head_count, TILE, HD), jnp.float32),
             ],
         ),

time: 221 us -> 219 us (level)
  no operation moved by 1% of the time
where the time goes in v4:
time: 219 us; the launch traced here: 217 us
  waiting for transfers between devices  151 us (69%)
  blocking collectives  33.7 us (15%)
  Pallas kernels  13.5 us (6%)
  between operations  13.4 us (6%)
  other arithmetic  4.62 us (2%)
    all_gather x1, waiting for transfers between devices, shards(): lax.all_gather(jnp.concatenate([key_vectors, value_vectors], axis=1), 'fr...  151 us
    all_to_all x1, blocking collectives, shards(): lax.all_to_all(partial.reshape(head_count, row_count // head_count, parti...  33.7 us
    pallas_call x1, Pallas kernels, sparse_attention(): pl.pallas_call(kernel, grid_spec=pltpu.PrefetchScalarGridSpec(num_scalar_...  13.5 us
  transfers between devices with their start and end apart: 1, of which 1 were waited for; matrix products, arithmetic and copies ran while one was open for 1% of the time, Pallas kernels for 0%

profile of v4, /device:TPU:1, one launch (start us, length us, event | category | flops | bytes accessed | tf_op | source)
XLA Modules:
  0.0 217.4 jit_solution(3702055503272653296)
XLA Ops:
  6.5 0.0 all-gather.2.cloned.1.call-start
  6.5 1.9 pad_maximum_fusion
  8.5 0.0 all-gather.2.cloned.1.call-update
  8.5 0.7 fusion.1
  9.2 0.3 reduce_window_sum.11
  9.5 0.2 fusion.2
  9.7 0.0 copy-start
  9.7 0.1 convert_reduce_fusion
  9.8 0.2 convert_reduce_fusion.1
  10.0 0.1 fusion
  10.1 0.6 select_n.13.lists_ref
  10.7 151.5 %all-gather.2.cloned.1.call-done.refs_0_.refs_1_.refs_2_.refs_3_.refs_4_.refs_5_.refs_6_.refs_7_.refs_8_.refs_9_.refs_10_.refs_11_.refs_12_.refs_13_.refs_14_.refs_15_.refs_16_.refs_17_ = bf16[12288,768]{1,0:T(8,128)(2,1)} async-done(((bf16[384,768]{1,0:T(8,128)(2,1)}), bf16[12288,768]{1,0:T(8,128)(2,1)}) %all-gather.2.cloned.1.call-update) | async-done | bytes 18874384 | tf_op jit(solution)/shard_map/all_gather | solution.py:132
  162.2 0.0 copy-done
  162.2 13.5 %shard_map.55 = bf16[384,3072]{1,0:T(8,128)(2,1)} custom-call(s32[81]{0:T(128)} %select_n.13.lists_ref, s32[3]{0:T(128)} %copy-done, bf16[384,384]{1,0:T(8,128)(2,1)} %q_ref.1, ...), custom_call_target="tpu_custom_call" | custom-call | tf_op jit(solution)/shard_map/pallas_call | solution.py:103
  175.7 33.7 %all_to_all.5 = bf16[8,48,3072]{2,1,0:T(8,128)(2,1)S(1)} all-to-all(bf16[8,48,3072]{2,1,0:T(8,128)(2,1)} %bitcast.1), channel_id=1, replica_groups=mesh['frame'=32,'head'=8] {'head'}, dimensions={0} | all-to-all | bytes 4718592 | tf_op jit(solution)/shard_map/all_to_all | solution.py:137
  209.4 1.1 reduce_sum.32
Async XLA Ops:
  6.5 155.6 %all-gather.2.cloned.1.call-start = ((), (), s32[]{:S(2)}) async-start(), calls=%async_computation.1 | async-start | bytes 19464192 | tf_op jit(solution)/shard_map/all_gather | solution.py:132
  9.7 152.5 %copy-start = (s32[3]{0:T(128)}, s32[3]{0:T(128)S(1)}, u32[]{:S(2)}) copy-start(s32[3]{0:T(128)S(1)} %get-tuple-element.5.counts_ref) | copy-start | bytes 40
Sparse Core Ops, SparseCore 0:
  10.1 152.0 all-gather.1

commit v5 on v3

--- a/solution.py
+++ b/solution.py
@@ -40,8 +40,8 @@
         acc_ref[...] = jnp.zeros(acc_ref.shape, jnp.float32)
 
     def update(masked):
-        column = lax.broadcasted_iota(jnp.int32, (1, KEYS_PER_STEP * TILE), 1)
-        in_list = column < valid * TILE
+        row = lax.broadcasted_iota(jnp.int32, (KEYS_PER_STEP * TILE, 1), 0)
+        in_list = row < valid * TILE
         for h in range(head_count):
             cols = pl.ds(h * HD, HD)
             q = q_ref[:, cols]
@@ -49,17 +49,18 @@
             k = jnp.concatenate([pair_refs[j][:, cols] for j in range(KEYS_PER_STEP)], axis=0)
             v = jnp.concatenate([pair_refs[j][:, value_cols] for j in range(KEYS_PER_STEP)], axis=0)
             s = lax.dot_general(
-                q, k, (((1,), (1,)), ((), ())), preferred_element_type=jnp.float32
+                k, q, (((1,), (1,)), ((), ())), preferred_element_type=jnp.float32
             ) * scale
             if masked:
                 s = jnp.where(in_list, s, -jnp.inf)
             old_top = top_ref[h]
-            new_top = jnp.maximum(old_top, jnp.max(s, axis=1, keepdims=True))
+            new_top = jnp.maximum(old_top, jnp.max(s, axis=0, keepdims=True))
             weights = jnp.exp(s - new_top)
             factor = jnp.exp(old_top - new_top)
-            total_ref[h] = total_ref[h] * factor + jnp.sum(weights, axis=1, keepdims=True)
-            acc_ref[h] = acc_ref[h] * factor + jnp.dot(
-                weights.astype(jnp.bfloat16), v, preferred_element_type=jnp.float32
+            total_ref[h] = total_ref[h] * factor + jnp.sum(weights, axis=0, keepdims=True)
+            acc_ref[h] = acc_ref[h] * factor + lax.dot_general(
+                v, weights.astype(jnp.bfloat16), (((0,), (0,)), ((), ())),
+                preferred_element_type=jnp.float32,
             )
             top_ref[h] = new_top
 
@@ -74,7 +75,7 @@
     @pl.when(step == pl.num_programs(1) - 1)
     def _():
         attended = jnp.concatenate(
-            [(acc_ref[h] / total_ref[h]).astype(jnp.bfloat16) for h in range(head_count)], axis=1
+            [(acc_ref[h] / total_ref[h]).T.astype(jnp.bfloat16) for h in range(head_count)], axis=1
         )
         o_ref[...] = jnp.dot(attended, w_ref[...], preferred_element_type=jnp.float32).astype(
             o_ref.dtype
@@ -112,8 +113,8 @@
                 (TILE, out_weight.shape[1]), lambda i, s, lists_ref, counts_ref: (i, 0)
             ),
             scratch_shapes=[
-                pltpu.VMEM((head_count, TILE, 1), jnp.float32),
-                pltpu.VMEM((head_count, TILE, 1), jnp.float32),
+                pltpu.VMEM((head_count, 1, TILE), jnp.float32),
+                pltpu.VMEM((head_count, 1, TILE), jnp.float32),
                 pltpu.VMEM((head_count, TILE, HD), jnp.float32),
             ],
         ),

time: 220 us -> 218 us (level)
  Pallas kernels: 15.5 us -> 13.1 us
    pallas_call x1, Pallas kernels: 15.5 us -> 13.1 us  [sparse_attention(): pl.pallas_call(kernel, grid_spec=pltpu.PrefetchScalarGridSpec(num_scalar_...]
where the time goes in v5:
time: 218 us; the launch traced here: 217 us
  waiting for transfers between devices  151 us (69%)
  blocking collectives  33.6 us (15%)
  between operations  13.4 us (6%)
  Pallas kernels  13.1 us (6%)
  other arithmetic  4.62 us (2%)
    all_gather x1, waiting for transfers between devices, shards(): lax.all_gather(jnp.concatenate([key_vectors, value_vectors], axis=1), 'fr...  151 us
    all_to_all x1, blocking collectives, shards(): lax.all_to_all(partial.reshape(head_count, row_count // head_count, parti...  33.6 us
    pallas_call x1, Pallas kernels, sparse_attention(): pl.pallas_call(kernel, grid_spec=pltpu.PrefetchScalarGridSpec(num_scalar_...  13.1 us
  transfers between devices with their start and end apart: 1, of which 1 were waited for; matrix products, arithmetic and copies ran while one was open for 1% of the time, Pallas kernels for 0%

profile of v5, /device:TPU:1, one launch (start us, length us, event | category | flops | bytes accessed | tf_op | source)
XLA Modules:
  0.0 216.8 jit_solution(9763234018858842215)
XLA Ops:
  6.5 0.0 all-gather.2.cloned.1.call-start
  6.5 1.9 pad_maximum_fusion
  8.5 0.0 all-gather.2.cloned.1.call-update
  8.5 0.7 fusion.1
  9.2 0.3 reduce_window_sum.11
  9.5 0.2 fusion.2
  9.7 0.0 copy-start
  9.7 0.1 convert_reduce_fusion
  9.8 0.2 convert_reduce_fusion.1
  10.0 0.1 fusion
  10.1 0.6 select_n.13.lists_ref
  10.7 151.5 %all-gather.2.cloned.1.call-done.refs_0_.refs_1_.refs_2_.refs_3_.refs_4_.refs_5_.refs_6_.refs_7_.refs_8_ = bf16[12288,768]{1,0:T(8,128)(2,1)} async-done(((bf16[384,768]{1,0:T(8,128)(2,1)}), bf16[12288,768]{1,0:T(8,128)(2,1)}) %all-gather.2.cloned.1.call-update) | async-done | bytes 18874384 | tf_op jit(solution)/shard_map/all_gather | solution.py:132
  162.2 0.0 copy-done
  162.2 13.1 %shard_map.55 = bf16[384,3072]{1,0:T(8,128)(2,1)} custom-call(s32[81]{0:T(128)} %select_n.13.lists_ref, s32[3]{0:T(128)} %copy-done, bf16[384,384]{1,0:T(8,128)(2,1)} %q_ref.1, bf16[12288,768]{1,0:T(8,128)(2,1)} %all-gather.2.cloned.1.call-done.refs_0_.refs_1_.refs_2_.refs_3_.refs_4_.refs_5_.refs_6_.refs_7_.refs_8_, ...), custom_call_target="tpu_custom_call" | custom-call | tf_op jit(solution)/shard_map/pallas_call | solution.py:104
  175.3 33.6 %all_to_all.5 = bf16[8,48,3072]{2,1,0:T(8,128)(2,1)S(1)} all-to-all(bf16[8,48,3072]{2,1,0:T(8,128)(2,1)} %bitcast.1), channel_id=1, replica_groups=mesh['frame'=32,'head'=8] {'head'}, dimensions={0} | all-to-all | bytes 4718592 | tf_op jit(solution)/shard_map/all_to_all | solution.py:137
  208.9 1.1 reduce_sum.32
Async XLA Ops:
  6.5 155.6 %all-gather.2.cloned.1.call-start = ((), (), s32[]{:S(2)}) async-start(), calls=%async_computation.1 | async-start | bytes 19464192 | tf_op jit(solution)/shard_map/all_gather | solution.py:132
  9.7 152.5 %copy-start = (s32[3]{0:T(128)}, s32[3]{0:T(128)S(1)}, u32[]{:S(2)}) copy-start(s32[3]{0:T(128)S(1)} %get-tuple-element.5.counts_ref) | copy-start | bytes 40
Sparse Core Ops, SparseCore 0:
  10.1 152.0 all-gather.1

commit v6 on v5

--- a/solution.py
+++ b/solution.py
@@ -11,13 +11,14 @@
 HD = 128
 TILE = 128
 MAX_KEYS = 27
-KEYS_PER_STEP = 9
+KEYS_PER_STEP = 18
+SLOTS = 36
 
 
 def key_lists(tile_rows):
     seen = jnp.cumsum((tile_rows > 0).astype(jnp.int32), axis=1)
     counts = jnp.minimum(seen[:, -1], MAX_KEYS)
-    slots = jnp.arange(MAX_KEYS, dtype=jnp.int32)
+    slots = jnp.arange(SLOTS, dtype=jnp.int32)
     lists = jnp.sum((seen[:, None, :] <= slots[None, :, None]).astype(jnp.int32), axis=2)
     last = jnp.sum((seen <= (counts - 1)[:, None]).astype(jnp.int32), axis=1)
     lists = jnp.where(slots[None, :] < counts[:, None], lists, last[:, None])
@@ -86,13 +87,13 @@
     row_count, channels = query_vectors.shape
     head_count = channels // HD
     query_tiles = row_count // TILE
-    steps = MAX_KEYS // KEYS_PER_STEP
+    steps = SLOTS // KEYS_PER_STEP
 
     def key_spec(j):
         return pl.BlockSpec(
             (TILE, 2 * channels),
             lambda i, s, lists_ref, counts_ref: (
-                lists_ref[i * MAX_KEYS + s * KEYS_PER_STEP + j],
+                lists_ref[i * SLOTS + s * KEYS_PER_STEP + j],
                 0,
             ),
         )

time: 218 us -> 222 us (1.018)
  Pallas kernels: 13.1 us -> 18.1 us
    pallas_call x1, Pallas kernels: 13.1 us -> 18.1 us  [sparse_attention(): pl.pallas_call(kernel, grid_spec=pltpu.PrefetchScalarGridSpec(num_scalar_...]
where the time goes in v6:
time: 222 us; the launch traced here: 221 us
  waiting for transfers between devices  151 us (68%)
  blocking collectives  33.2 us (15%)
  Pallas kernels  18.1 us (8%)
  between operations  13.4 us (6%)
  other arithmetic  4.62 us (2%)
    all_gather x1, waiting for transfers between devices, shards(): lax.all_gather(jnp.concatenate([key_vectors, value_vectors], axis=1), 'fr...  151 us
    all_to_all x1, blocking collectives, shards(): lax.all_to_all(partial.reshape(head_count, row_count // head_count, parti...  33.2 us
    pallas_call x1, Pallas kernels, sparse_attention(): pl.pallas_call(kernel, grid_spec=pltpu.PrefetchScalarGridSpec(num_scalar_...  18.1 us
  transfers between devices with their start and end apart: 1, of which 1 were waited for; matrix products, arithmetic and copies ran while one was open for 1% of the time, Pallas kernels for 0%

profile of v6, /device:TPU:1, one launch (start us, length us, event | category | flops | bytes accessed | tf_op | source)
XLA Modules:
  0.0 221.4 jit_solution(2896086392233945486)
XLA Ops:
  6.5 0.0 all-gather.2.cloned.1.call-start
  6.5 1.9 pad_maximum_fusion
  8.5 0.0 all-gather.2.cloned.1.call-update
  8.5 0.7 fusion.1
  9.2 0.3 reduce_window_sum.11
  9.5 0.2 fusion.2
  9.7 0.0 copy-start
  9.7 0.1 convert_reduce_fusion
  9.8 0.2 convert_reduce_fusion.1
  10.0 0.1 fusion
  10.1 0.6 select_n.13.lists_ref
  10.7 151.5 %all-gather.2.cloned.1.call-done.refs_0_.refs_1_.refs_2_.refs_3_.refs_4_.refs_5_.refs_6_.refs_7_.refs_8_.refs_9_.refs_10_.refs_11_.refs_12_.refs_13_.refs_14_.refs_15_.refs_16_.refs_17_ = bf16[12288,768]{1,0:T(8,128)(2,1)} async-done(((bf16[384,768]{1,0:T(8,128)(2,1)}), bf16[12288,768]{1,0:T(8,128)(2,1)}) %all-gather.2.cloned.1.call-update) | async-done | bytes 18874384 | tf_op jit(solution)/shard_map/all_gather | solution.py:133
  162.2 0.0 copy-done
  162.2 18.1 %shard_map.55 = bf16[384,3072]{1,0:T(8,128)(2,1)} custom-call(s32[108]{0:T(128)} %select_n.13.lists_ref, s32[3]{0:T(128)} %copy-done, bf16[384,384]{1,0:T(8,128)(2,1)} %q_ref.1, ...), custom_call_target="tpu_custom_call" | custom-call | tf_op jit(solution)/shard_map/pallas_call | solution.py:105
  180.3 33.2 %all_to_all.5 = bf16[8,48,3072]{2,1,0:T(8,128)(2,1)S(1)} all-to-all(bf16[8,48,3072]{2,1,0:T(8,128)(2,1)} %bitcast.1), channel_id=1, replica_groups=mesh['frame'=32,'head'=8] {'head'}, dimensions={0} | all-to-all | bytes 4718592 | tf_op jit(solution)/shard_map/all_to_all | solution.py:138
  213.5 1.1 reduce_sum.32
Async XLA Ops:
  6.5 155.6 %all-gather.2.cloned.1.call-start = ((), (), s32[]{:S(2)}) async-start(), calls=%async_computation.1 | async-start | bytes 19464192 | tf_op jit(solution)/shard_map/all_gather | solution.py:133
  9.7 152.5 %copy-start = (s32[3]{0:T(128)}, s32[3]{0:T(128)S(1)}, u32[]{:S(2)}) copy-start(s32[3]{0:T(128)S(1)} %get-tuple-element.5.counts_ref) | copy-start | bytes 40
Sparse Core Ops, SparseCore 0:
  10.1 152.0 all-gather.1

commit v7 on v6

--- a/solution.py
+++ b/solution.py
@@ -11,8 +11,8 @@
 HD = 128
 TILE = 128
 MAX_KEYS = 27
-KEYS_PER_STEP = 18
-SLOTS = 36
+KEYS_PER_STEP = 6
+SLOTS = 30
 
 
 def key_lists(tile_rows):

time: 222 us -> 219 us (0.986); the launches traced: 221 us -> 216 us
  Pallas kernels: 18.1 us -> 12.2 us
    pallas_call x1, Pallas kernels: 18.1 us -> 12.2 us  [sparse_attention(): pl.pallas_call(kernel, grid_spec=pltpu.PrefetchScalarGridSpec(num_scalar_...]
where the time goes in v7:
time: 219 us; the launch traced here: 216 us
  waiting for transfers between devices  151 us (69%)
  blocking collectives  33.5 us (15%)
  between operations  13.4 us (6%)
  Pallas kernels  12.2 us (6%)
  other arithmetic  4.62 us (2%)
    all_gather x1, waiting for transfers between devices, shards(): lax.all_gather(jnp.concatenate([key_vectors, value_vectors], axis=1), 'fr...  151 us
    all_to_all x1, blocking collectives, shards(): lax.all_to_all(partial.reshape(head_count, row_count // head_count, parti...  33.5 us
    pallas_call x1, Pallas kernels, sparse_attention(): pl.pallas_call(kernel, grid_spec=pltpu.PrefetchScalarGridSpec(num_scalar_...  12.2 us
  transfers between devices with their start and end apart: 1, of which 1 were waited for; matrix products, arithmetic and copies ran while one was open for 1% of the time, Pallas kernels for 0%

profile of v7, /device:TPU:1, one launch (start us, length us, event | category | flops | bytes accessed | tf_op | source)
XLA Modules:
  0.0 215.9 jit_solution(4262171347342308331)
XLA Ops:
  6.5 0.0 all-gather.2.cloned.1.call-start
  6.5 1.9 pad_maximum_fusion
  8.5 0.0 all-gather.2.cloned.1.call-update
  8.5 0.7 fusion.1
  9.2 0.3 reduce_window_sum.11
  9.5 0.2 fusion.2
  9.7 0.0 copy-start
  9.7 0.1 convert_reduce_fusion
  9.8 0.2 convert_reduce_fusion.1
  10.0 0.1 fusion
  10.1 0.6 select_n.13.lists_ref
  10.7 151.5 %all-gather.2.cloned.1.call-done.refs_0_.refs_1_.refs_2_.refs_3_.refs_4_.refs_5_ = bf16[12288,768]{1,0:T(8,128)(2,1)} async-done(((bf16[384,768]{1,0:T(8,128)(2,1)}), bf16[12288,768]{1,0:T(8,128)(2,1)}) %all-gather.2.cloned.1.call-update) | async-done | bytes 18874384 | tf_op jit(solution)/shard_map/all_gather | solution.py:133
  162.2 0.0 copy-done
  162.2 12.2 %shard_map.55 = bf16[384,3072]{1,0:T(8,128)(2,1)} custom-call(s32[90]{0:T(128)} %select_n.13.lists_ref, s32[3]{0:T(128)} %copy-done, bf16[384,384]{1,0:T(8,128)(2,1)} %q_ref.1, bf16[12288,768]{1,0:T(8,128)(2,1)} %all-gather.2.cloned.1.call-done.refs_0_.refs_1_.refs_2_.refs_3_.refs_4_.refs_5_, ...), custom_call_target="tpu_custom_call" | custom-call | tf_op jit(solution)/shard_map/pallas_call | solution.py:105
  174.4 33.5 %all_to_all.5 = bf16[8,48,3072]{2,1,0:T(8,128)(2,1)S(1)} all-to-all(bf16[8,48,3072]{2,1,0:T(8,128)(2,1)} %bitcast.1), channel_id=1, replica_groups=mesh['frame'=32,'head'=8] {'head'}, dimensions={0} | all-to-all | bytes 4718592 | tf_op jit(solution)/shard_map/all_to_all | solution.py:138
  207.9 1.1 reduce_sum.32
Async XLA Ops:
  6.5 155.6 %all-gather.2.cloned.1.call-start = ((), (), s32[]{:S(2)}) async-start(), calls=%async_computation.1 | async-start | bytes 19464192 | tf_op jit(solution)/shard_map/all_gather | solution.py:133
  9.7 152.5 %copy-start = (s32[3]{0:T(128)}, s32[3]{0:T(128)S(1)}, u32[]{:S(2)}) copy-start(s32[3]{0:T(128)S(1)} %get-tuple-element.5.counts_ref) | copy-start | bytes 40
Sparse Core Ops, SparseCore 0:
  10.1 152.0 all-gather.1

commit v8 on v5

--- a/solution.py
+++ b/solution.py
@@ -26,12 +26,17 @@
 
 def attention_kernel(lists_ref, counts_ref, q_ref, *refs, head_count, scale):
     pair_refs = refs[:KEYS_PER_STEP]
-    w_ref, o_ref = refs[KEYS_PER_STEP : KEYS_PER_STEP + 2]
-    top_ref, total_ref, acc_ref = refs[KEYS_PER_STEP + 2 :]
+    w_hbm, o_ref = refs[KEYS_PER_STEP : KEYS_PER_STEP + 2]
+    top_ref, total_ref, acc_ref, w_ref, w_sem = refs[KEYS_PER_STEP + 2 :]
     channels = q_ref.shape[1]
     tile = pl.program_id(0)
     step = pl.program_id(1)
     valid = counts_ref[tile] - step * KEYS_PER_STEP
+    weight_copy = pltpu.make_async_copy(w_hbm, w_ref, w_sem)
+
+    @pl.when((tile == 0) & (step == 0))
+    def _():
+        weight_copy.start()
 
     @pl.when(step == 0)
     def _():
@@ -72,6 +77,10 @@
     def _():
         update(True)
 
+    @pl.when((tile == 0) & (step == pl.num_programs(1) - 1))
+    def _():
+        weight_copy.wait()
+
     @pl.when(step == pl.num_programs(1) - 1)
     def _():
         attended = jnp.concatenate(
@@ -108,7 +117,7 @@
             grid=(query_tiles, steps),
             in_specs=[row_spec]
             + [key_spec(j) for j in range(KEYS_PER_STEP)]
-            + [pl.BlockSpec(out_weight.shape, lambda i, s, lists_ref, counts_ref: (0, 0))],
+            + [pl.BlockSpec(memory_space=pl.ANY)],
             out_specs=pl.BlockSpec(
                 (TILE, out_weight.shape[1]), lambda i, s, lists_ref, counts_ref: (i, 0)
             ),
@@ -116,6 +125,8 @@
                 pltpu.VMEM((head_count, 1, TILE), jnp.float32),
                 pltpu.VMEM((head_count, 1, TILE), jnp.float32),
                 pltpu.VMEM((head_count, TILE, HD), jnp.float32),
+                pltpu.VMEM(out_weight.shape, out_weight.dtype),
+                pltpu.SemaphoreType.DMA(()),
             ],
         ),
         out_shape=jax.ShapeDtypeStruct((row_count, out_weight.shape[1]), jnp.bfloat16),

time: 218 us -> 216 us (level)
  no operation moved by 1% of the time
where the time goes in v8:
time: 216 us; the launch traced here: 215 us
  waiting for transfers between devices  151 us (70%)
  blocking collectives  33.1 us (15%)
  between operations  13.4 us (6%)
  Pallas kernels  11.9 us (6%)
  other arithmetic  4.62 us (2%)
    all_gather x1, waiting for transfers between devices, shards(): lax.all_gather(jnp.concatenate([key_vectors, value_vectors], axis=1), 'fr...  151 us
    all_to_all x1, blocking collectives, shards(): lax.all_to_all(partial.reshape(head_count, row_count // head_count, parti...  33.1 us
    pallas_call x1, Pallas kernels, sparse_attention(): pl.pallas_call(kernel, grid_spec=pltpu.PrefetchScalarGridSpec(num_scalar_...  11.9 us
  transfers between devices with their start and end apart: 1, of which 1 were waited for; matrix products, arithmetic and copies ran while one was open for 1% of the time, Pallas kernels for 0%

profile of v8, /device:TPU:1, one launch (start us, length us, event | category | flops | bytes accessed | tf_op | source)
XLA Modules:
  0.0 215.1 jit_solution(16710971720044801673)
XLA Ops:
  6.5 0.0 all-gather.2.cloned.1.call-start
  6.5 1.9 pad_maximum_fusion
  8.5 0.0 all-gather.2.cloned.1.call-update
  8.5 0.7 fusion.1
  9.2 0.3 reduce_window_sum.11
  9.5 0.2 fusion.2
  9.7 0.0 copy-start
  9.7 0.1 convert_reduce_fusion
  9.8 0.2 convert_reduce_fusion.1
  10.0 0.1 fusion
  10.1 0.6 select_n.13.lists_ref
  10.7 151.5 %all-gather.2.cloned.1.call-done.refs_0_.refs_1_.refs_2_.refs_3_.refs_4_.refs_5_.refs_6_.refs_7_.refs_8_ = bf16[12288,768]{1,0:T(8,128)(2,1)} async-done(((bf16[384,768]{1,0:T(8,128)(2,1)}), bf16[12288,768]{1,0:T(8,128)(2,1)}) %all-gather.2.cloned.1.call-update) | async-done | bytes 18874384 | tf_op jit(solution)/shard_map/all_gather | solution.py:143
  162.2 0.0 copy-done
  162.2 11.9 %shard_map.55 = bf16[384,3072]{1,0:T(8,128)(2,1)} custom-call(s32[81]{0:T(128)} %select_n.13.lists_ref, s32[3]{0:T(128)} %copy-done, bf16[384,384]{1,0:T(8,128)(2,1)} %q_ref.1, bf16[12288,768]{1,0:T(8,128)(2,1)} %all-gather.2.cloned.1.call-done.refs_0_.refs_1_.refs_2_.refs_3_.refs_4_.refs_5_.refs_6_.refs_7_.refs_8_, ...), custom_call_target="tpu_custom_call" | custom-call | tf_op jit(solution)/shard_map/pallas_call | solution.py:113
  174.0 33.1 %all_to_all.5 = bf16[8,48,3072]{2,1,0:T(8,128)(2,1)S(1)} all-to-all(bf16[8,48,3072]{2,1,0:T(8,128)(2,1)} %bitcast.1), channel_id=1, replica_groups=mesh['frame'=32,'head'=8] {'head'}, dimensions={0} | all-to-all | bytes 4718592 | tf_op jit(solution)/shard_map/all_to_all | solution.py:148
  207.1 1.1 reduce_sum.32
Async XLA Ops:
  6.5 155.6 %all-gather.2.cloned.1.call-start = ((), (), s32[]{:S(2)}) async-start(), calls=%async_computation.1 | async-start | bytes 19464192 | tf_op jit(solution)/shard_map/all_gather | solution.py:143
  9.7 152.5 %copy-start = (s32[3]{0:T(128)}, s32[3]{0:T(128)S(1)}, u32[]{:S(2)}) copy-start(s32[3]{0:T(128)S(1)} %get-tuple-element.5.counts_ref) | copy-start | bytes 40
Sparse Core Ops, SparseCore 0:
  10.1 152.0 all-gather.1
